TPU v7x, 128 devices: a whole 4x4x4 slice. The times are simulated.
128 devices in a mesh: node: 4 (over x), ep: 32 (over y, z, core).
Axes of the slice: x: 4, y: 4, z: 4, core: 2. Of those that a mesh axis runs over, the one named last changes fastest.
Arguments:
- images: bfloat16 [128, 257, 1280], P(('node', 'ep')), may hold values from -6 to 6
- w_query: bfloat16 [1280, 1280], P(None, 'node'), may hold values from -6 to 6
- w_key: bfloat16 [1280, 1280], P(None, 'node'), may hold values from -6 to 6
- w_value: bfloat16 [1280, 1280], P(None, 'node'), may hold values from -0.15625 to 0.15625
- w_output: bfloat16 [1280, 1280], replicated, may hold values from -0.15625 to 0.15625
- router: bfloat16 [1280, 32], replicated, may hold values from -0.15625 to 0.15625
- w_in: bfloat16 [32, 1280, 5120], P('ep', None, 'node'), may hold values from -0.15625 to 0.15625
- w_out: bfloat16 [32, 5120, 1280], P('ep', 'node'), may hold values from -0.078125 to 0.078125
- routes: int32 [128, 257, 2], P(('node', 'ep')), may hold values from 0 to 31, all different within a row; in each aligned block of 257 rows (0 to 256, 257 to 513, ..., all dimensions but the last counted through in order) at most 24 rows name the same one
Outputs:
- output: bfloat16 [128, 257, 1280], P(('node', 'ep'))
Inputs may be any that keep to these rules, and one draw needn't show every extreme that they name: `routes`: the two experts of a token differ. At most 24 tokens of one image name the same expert, and in every draw some image has an expert named by exactly 24 of its tokens.
All inputs are finite; a program needn't handle non-finite values.
Results may differ from a plain program's by a relative error of at most 0.0085.
Values may be sent and summed in bfloat16 or wider, within the bound.
No kernel may reach another device: no remote copies, remote signals or barrier semaphores. Data moves between devices by JAX's collectives and lax.ppermute only.
A program may use at most 128 MiB of HBM per device.

v0:
```python
import math

import jax
import jax.numpy as jnp
from jax import lax
from jax.sharding import PartitionSpec as P

D = 1280
HEADS = 16
CAP = 24


def layer_norm(values):
    center = values - jnp.mean(values, axis=-1, keepdims=True)
    spread = jnp.mean(center * center, axis=-1, keepdims=True)
    return center * lax.rsqrt(spread + 1e-06)


def slot_table(chosen, num_experts):
    onehot = (chosen[..., None] == jnp.arange(num_experts, dtype=jnp.int32)).astype(jnp.int32)
    before = jnp.cumsum(onehot, axis=1) - onehot
    return jnp.sum(before * onehot, axis=-1)


def shards(images, w_query, w_key, w_value, w_output, router, w_in, w_out, routes):
    local_images, tokens_dev, width = images.shape
    head_size = D // HEADS
    local_heads = w_query.shape[1] // head_size
    node_count = lax.axis_size("node")
    column_count = lax.axis_size("ep")
    num_experts = router.shape[1]
    local_experts = w_in.shape[0]
    slot_count = local_images * CAP
    inputs = images.astype(jnp.float32)
    normed = layer_norm(inputs).astype(jnp.bfloat16)
    node_index = lax.axis_index("node")
    ahead = [(i, (i + 1) % node_count) for i in range(node_count)]
    behind = [(i, (i - 1) % node_count) for i in range(node_count)]
    split = width // 2
    from_behind = lax.ppermute(normed, "node", ahead)
    from_ahead = lax.ppermute(normed, "node", behind)
    far = jnp.concatenate(
        [
            lax.ppermute(from_behind[..., :split], "node", ahead),
            lax.ppermute(from_ahead[..., split:], "node", behind),
        ],
        axis=-1,
    )
    shard_rows = jnp.concatenate([normed, from_ahead, far, from_behind], axis=0)
    number = shard_rows.shape[0]
    queries = jnp.einsum(
        "ctd,de->cet", shard_rows, w_query, preferred_element_type=jnp.float32
    ).astype(jnp.bfloat16)
    projected_keys = jnp.einsum(
        "ctd,de->cet", shard_rows, w_key, preferred_element_type=jnp.float32
    ).astype(jnp.bfloat16)
    projected_values = jnp.einsum(
        "ctd,de->cet", shard_rows, w_value, preferred_element_type=jnp.float32
    ).astype(jnp.bfloat16)
    query_heads = queries.reshape(number, local_heads, head_size, tokens_dev)
    key_heads = projected_keys.reshape(number, local_heads, head_size, tokens_dev)
    value_heads = projected_values.reshape(number, local_heads, head_size, tokens_dev)
    scores = jnp.einsum(
        "chdq,chdk->chqk", query_heads, key_heads, preferred_element_type=jnp.float32
    ) / math.sqrt(head_size)
    weights = jax.nn.softmax(scores, axis=-1).astype(jnp.bfloat16)
    mixture = jnp.einsum(
        "chqk,chdk->cqhd", weights, value_heads, preferred_element_type=jnp.float32
    ).astype(jnp.bfloat16)
    head_results = jnp.roll(mixture.reshape(number, tokens_dev, local_heads * head_size), node_index, axis=0)
    exchanged = lax.all_to_all(head_results, "node", split_axis=0, concat_axis=0, tiled=True)
    attention = jnp.einsum(
        "gtd,gde->te",
        exchanged,
        w_output.reshape(node_count, local_heads * head_size, width),
        preferred_element_type=jnp.float32,
    ).reshape(local_images, tokens_dev, width)
    middle = inputs + attention
    normed_second = layer_norm(middle).astype(jnp.bfloat16)
    logits = jnp.einsum("itd,de->ite", normed_second, router, preferred_element_type=jnp.float32)
    chosen_mask = routes[..., None] == jnp.arange(num_experts, dtype=jnp.int32)
    chosen_logit = jnp.sum(jnp.where(chosen_mask, logits[:, :, None, :], jnp.float32(0.0)), axis=-1)
    gate_values = jax.nn.sigmoid(chosen_logit)
    flat_routes = routes.reshape(local_images, 2 * tokens_dev)
    slot_index = slot_table(flat_routes, num_experts)
    image_base = jnp.arange(local_images, dtype=jnp.int32)[:, None] * CAP
    position = (flat_routes * slot_count + image_base + slot_index).reshape(-1)
    token_count = local_images * tokens_dev
    token_slots = position.reshape(token_count, 2)
    slot_ids = jnp.arange(num_experts * slot_count, dtype=jnp.int32)
    token_rows = normed_second.reshape(token_count, width)
    hits = (token_slots[None, :, 0] == slot_ids[:, None]) | (token_slots[None, :, 1] == slot_ids[:, None])
    gathered = jnp.dot(
        hits.astype(jnp.bfloat16), token_rows, preferred_element_type=jnp.float32
    ).astype(jnp.bfloat16)
    outgoing = gathered.reshape(column_count, local_experts, slot_count, width)
    bounds = [0, slot_count // 3, slot_count]
    pieces = []
    for low, high in zip(bounds[:-1], bounds[1:]):
        chunk = high - low
        sent = outgoing[:, :, low:high, :]
        block = lax.all_to_all(sent, "ep", split_axis=0, concat_axis=0, tiled=True).reshape(-1, width)
        half = block.shape[0] // 2
        came_behind = lax.ppermute(block, "node", ahead)
        came_ahead = lax.ppermute(block, "node", behind)
        came_far = jnp.concatenate(
            [
                lax.ppermute(came_behind[:half], "node", ahead),
                lax.ppermute(came_ahead[half:], "node", behind),
            ],
            axis=0,
        )
        rows = jnp.concatenate([block, came_ahead, came_far, came_behind], axis=0)
        pre_act = jnp.dot(rows, w_in[0], preferred_element_type=jnp.float32)
        hidden = jax.nn.gelu(pre_act, approximate=True).astype(jnp.bfloat16)
        partial_sum = jnp.dot(hidden, w_out[0], preferred_element_type=jnp.float32).astype(jnp.bfloat16)
        own_part, next_part, far_part, prev_part = jnp.split(partial_sum, node_count, axis=0)
        got_low = lax.ppermute(far_part[:half], "node", ahead).astype(jnp.float32)
        got_high = lax.ppermute(far_part[half:], "node", behind).astype(jnp.float32)
        to_next = jnp.concatenate(
            [next_part[:half].astype(jnp.float32) + got_low, next_part[half:].astype(jnp.float32)], axis=0
        )
        to_prev = jnp.concatenate(
            [prev_part[:half].astype(jnp.float32), prev_part[half:].astype(jnp.float32) + got_high], axis=0
        )
        back_behind = lax.ppermute(to_next.astype(jnp.bfloat16), "node", ahead)
        back_ahead = lax.ppermute(to_prev.astype(jnp.bfloat16), "node", behind)
        summed = (
            own_part.astype(jnp.float32) + back_behind.astype(jnp.float32) + back_ahead.astype(jnp.float32)
        ).astype(jnp.bfloat16)
        summed = summed.reshape(column_count, local_experts, chunk, width)
        pieces.append(lax.all_to_all(summed, "ep", split_axis=0, concat_axis=0, tiled=True))
    expert_result = jnp.concatenate(pieces, axis=2)
    result_rows = expert_result.reshape(num_experts * slot_count, width)
    flat_gates = gate_values.reshape(token_count, 2)
    combine = jnp.where(token_slots[:, 0:1] == slot_ids[None, :], flat_gates[:, 0:1], jnp.float32(0.0)) + jnp.where(
        token_slots[:, 1:2] == slot_ids[None, :], flat_gates[:, 1:2], jnp.float32(0.0)
    )
    expert_mix = jnp.dot(
        combine, result_rows.astype(jnp.float32), precision=lax.Precision.HIGHEST,
        preferred_element_type=jnp.float32,
    ).reshape(local_images, tokens_dev, width)
    return (middle + expert_mix).astype(jnp.bfloat16)


def solution(mesh):
    placed = (
        P(("node", "ep"), None, None),
        P(None, "node"),
        P(None, "node"),
        P(None, "node"),
        P(),
        P(),
        P("ep", None, "node"),
        P("ep", "node", None),
        P(("node", "ep"), None, None),
    )
    return jax.shard_map(
        shards, mesh=mesh, in_specs=placed, out_specs=P(("node", "ep"), None, None), check_vma=False
    )
```

profile of v0, /device:TPU:1, one launch (start us, length us, event | category | flops | bytes accessed | tf_op | source)
XLA Modules:
  0.0 353.9 jit_solution(7066671258735016948)
XLA Ops:
  9.4 3.0 reduce-window.6
  12.4 10.9 %collective-permute-done.1 = bf16[1,257,1280]{2,1,0:T(8,128)(2,1)} collective-permute-done((bf16[1,257,1280]{2,1,0:T(8,128)(2,1)}, bf16[1,257,1280]{2,1,0:T(8,128)(2,1)}, u32[]{:S(2)}, u32[]{:S(2)}) %collective-permute-start.1) | collective-permute-done | bytes 657952 | tf_op jit(solution)/shard_map/ppermute | solution.py:40
  35.1 4.5 %fusion.48 = bf16[4,320,257]{1,2,0:T(8,128)(2,1)} fusion(bf16[1280,320]{0,1:T(8,128)(2,1)} %param.10, bf16[1,257,1280]{2,1,0:T(8,128)(2,1)} %collective-permute-done.1, bf16[1,257,640]{2,1,0:T(8,128)(2,1)} %collective-permute-done.3, bf16[1,257,640]{2,1,0:T(8,128)(2,1)} %collective-permute-done.2, bf16[1,257,1280]{2,1,0:T(8,128)(2,1)} %collective-permute-done, ...), kind=kOutput, calls=%fused_computation.66 | convolution fusion | flops 855624960 | bytes 4108800 | tf_op jit(solution)/shard_map/ctd,de->cet/dot_general | solution.py:51
  41.9 4.5 %fusion.47 = bf16[4,320,257]{1,2,0:T(8,128)(2,1)} fusion(bf16[1280,320]{0,1:T(8,128)(2,1)} %param.12, bf16[1,257,1280]{2,1,0:T(8,128)(2,1)} %collective-permute-done.1, bf16[1,257,640]{2,1,0:T(8,128)(2,1)} %collective-permute-done.3, bf16[1,257,640]{2,1,0:T(8,128)(2,1)} %collective-permute-done.2, bf16[1,257,1280]{2,1,0:T(8,128)(2,1)} %collective-permute-done, ...), kind=kOutput, calls=%fused_computation.65 | convolution fusion | flops 855624960 | bytes 4108800 | tf_op jit(solution)/shard_map/ctd,de->cet/dot_general | solution.py:57
  48.6 4.5 %fusion.49 = bf16[4,320,257]{1,2,0:T(8,128)(2,1)} fusion(bf16[1280,320]{0,1:T(8,128)(2,1)} %param.11, bf16[1,257,1280]{2,1,0:T(8,128)(2,1)} %collective-permute-done.1, bf16[1,257,640]{2,1,0:T(8,128)(2,1)} %collective-permute-done.3, bf16[1,257,640]{2,1,0:T(8,128)(2,1)} %collective-permute-done.2, bf16[1,257,1280]{2,1,0:T(8,128)(2,1)} %collective-permute-done, ...), kind=kOutput, calls=%fused_computation.67 | convolution fusion | flops 855624960 | bytes 4108800 | tf_op jit(solution)/shard_map/ctd,de->cet/dot_general | solution.py:54
  55.3 6.5 %fusion.87 = (f32[4,4,257]{2,1,0:T(4,128)S(1)}, f32[4,4,257,257]{2,3,1,0:T(8,128)}) fusion(bf16[4,4,80,257]{3,2,1,0:T(8,128)(2,1)} %bitcast.108, bf16[4,4,80,257]{3,2,1,0:T(8,128)(2,1)} %bitcast.109), kind=kOutput, calls=%fused_computation.138 | convolution fusion | flops 172256048 | bytes 5559424 | tf_op jit(solution)/shard_map/sub | solution.py:66
  61.8 5.1 %fusion.44 = bf16[4,4,80,257]{3,2,1,0:T(8,128)(2,1)} fusion(bf16[4,4,80,257]{3,2,1,0:T(8,128)(2,1)} %bitcast.107, f32[4,4,257,257]{2,3,1,0:T(8,128)} %get-tuple-element.22, f32[4,4,257]{2,1,0:T(4,128)S(1)} %get-tuple-element.21), kind=kOutput, calls=%fused_computation.52 | convolution fusion | flops 171527968 | bytes 5559424 | tf_op jit(solution)/shard_map/chqk,chdk->cqhd/dot_general | solution.py:67
  71.6 4.6 %all-to-all-start = ((bf16[4,257,320]{2,1,0:T(8,128)(2,1)}), bf16[4,257,320]{2,1,0:T(8,128)(2,1)}, u32[]{:S(2)}, u32[]{:S(2)}) async-start(bf16[4,257,320]{2,1,0:T(8,128)(2,1)} %fusion.57), calls=%async_computation | async-start | bytes 1622016 | tf_op jit(solution)/shard_map/all_to_all | solution.py:71
  77.6 8.2 %all-to-all-done = bf16[4,257,320]{2,1,0:T(8,128)(2,1)} async-done(((bf16[4,257,320]{2,1,0:T(8,128)(2,1)}), bf16[4,257,320]{2,1,0:T(8,128)(2,1)}, u32[]{:S(2)}, u32[]{:S(2)}) %all-to-all-start) | async-done | bytes 657952 | tf_op jit(solution)/shard_map/all_to_all | solution.py:71
  85.7 3.6 %fusion.88 = (f32[257]{0:T(512)S(1)}, f32[1,257,1280]{2,1,0:T(8,128)S(1)}) fusion(bf16[4,257,320]{2,1,0:T(8,128)(2,1)} %all-to-all-done, bf16[4,320,1280]{2,1,0:T(8,128)(2,1)} %bitcast.112, bf16[1,257,1280]{2,1,0:T(8,128)(2,1)} %param.9), kind=kOutput, calls=%fused_computation.139 | convolution fusion | flops 843124224 | bytes 5909508 | tf_op jit(solution)/shard_map/gtd,gde->te/dot_general | solution.py:72
  94.9 12.7 %all-to-all-start.1 = ((bf16[32,1,8,1280]{3,2,1,0:T(8,128)(2,1)}), bf16[32,1,8,1280]{3,2,1,0:T(8,128)(2,1)}, u32[]{:S(2)}, u32[]{:S(2)}) async-start(bf16[32,1,8,1280]{3,2,1,0:T(8,128)(2,1)} %slice.131), calls=%async_computation.1 | async-start | bytes 1310720 | tf_op jit(solution)/shard_map/all_to_all | solution.py:102
  107.6 2.5 slice.140
  110.1 10.5 %all-to-all-done.1 = bf16[32,1,8,1280]{3,2,1,0:T(8,128)(2,1)} async-done(((bf16[32,1,8,1280]{3,2,1,0:T(8,128)(2,1)}), bf16[32,1,8,1280]{3,2,1,0:T(8,128)(2,1)}, u32[]{:S(2)}, u32[]{:S(2)}) %all-to-all-start.1) | async-done | bytes 655392 | tf_op jit(solution)/shard_map/all_to_all | solution.py:102
  120.6 4.5 %all-to-all-start.3 = ((bf16[32,1,16,1280]{3,2,1,0:T(8,128)(2,1)}), bf16[32,1,16,1280]{3,2,1,0:T(8,128)(2,1)}, u32[]{:S(2)}, u32[]{:S(2)}) async-start(bf16[32,1,16,1280]{3,2,1,0:T(8,128)(2,1)} %slice.140), calls=%async_computation.3 | async-start | bytes 2621440 | tf_op jit(solution)/shard_map/all_to_all | solution.py:102
  129.8 14.8 %all-to-all-done.3 = bf16[32,1,16,1280]{3,2,1,0:T(8,128)(2,1)} async-done(((bf16[32,1,16,1280]{3,2,1,0:T(8,128)(2,1)}), bf16[32,1,16,1280]{3,2,1,0:T(8,128)(2,1)}, u32[]{:S(2)}, u32[]{:S(2)}) %all-to-all-start.3) | async-done | bytes 1310752 | tf_op jit(solution)/shard_map/all_to_all | solution.py:102
  151.9 2.7 collective-permute-start.7
  156.6 26.6 %collective-permute-done.6 = bf16[128,1280]{1,0:T(8,128)(2,1)S(1)} collective-permute-done((bf16[128,1280]{1,0:T(8,128)(2,1)S(1)}, bf16[128,1280]{1,0:T(8,128)(2,1)S(1)}, u32[]{:S(2)}, u32[]{:S(2)}) %collective-permute-start.6) | collective-permute-done | bytes 327712 | tf_op jit(solution)/shard_map/ppermute | solution.py:108
  186.7 10.9 %convolution_convert_fusion.1 = bf16[1024,1280]{1,0:T(8,128)(2,1)} fusion(bf16[1,1280,1280]{2,1,0:T(8,128)(2,1)S(1)} %copy-done, bf16[1024,1280]{1,0:T(8,128)(2,1)} %constant_dynamic-update-slice_fusion, bf16[1,1280,1280]{2,1,0:T(8,128)(2,1)} %param.15), kind=kOutput, calls=%fused_computation.28 | convolution fusion | flops 6723993600 | bytes 11796480 | tf_op jit(solution)/shard_map/dot_general | solution.py:116
  199.9 2.7 collective-permute-start.15
  205.0 2.7 collective-permute-start.10
  210.2 5.0 %collective-permute-done.14 = bf16[256,1280]{1,0:T(8,128)(2,1)S(1)} collective-permute-done((bf16[256,1280]{1,0:T(8,128)(2,1)S(1)}, bf16[256,1280]{1,0:T(8,128)(2,1)S(1)}, u32[]{:S(2)}, u32[]{:S(2)}) %collective-permute-start.14) | collective-permute-done | bytes 655392 | tf_op jit(solution)/shard_map/ppermute | solution.py:108
  219.4 18.6 %convolution_convert_fusion = bf16[2048,1280]{1,0:T(8,128)(2,1)} fusion(bf16[1,1280,1280]{2,1,0:T(8,128)(2,1)S(1)} %copy-done, bf16[2048,1280]{1,0:T(8,128)(2,1)} %constant_dynamic-update-slice_fusion.5, bf16[1,1280,1280]{2,1,0:T(8,128)(2,1)} %param.15), kind=kOutput, calls=%fused_computation.11 | convolution fusion | flops 13447987200 | bytes 17039360 | tf_op jit(solution)/shard_map/dot_general | solution.py:116
  240.1 2.8 collective-permute-start.18
  245.7 8.2 %collective-permute-done.16 = bf16[256,1280]{1,0:T(8,128)(2,1)S(1)} collective-permute-done((bf16[256,1280]{1,0:T(8,128)(2,1)S(1)}, bf16[256,1280]{1,0:T(8,128)(2,1)S(1)}, u32[]{:S(2)}, u32[]{:S(2)}) %collective-permute-start.16) | collective-permute-done | bytes 655392 | tf_op jit(solution)/shard_map/ppermute | solution.py:118
  260.5 6.5 %collective-permute-done.11 = bf16[256,1280]{1,0:T(8,128)(2,1)S(1)} collective-permute-done((bf16[256,1280]{1,0:T(8,128)(2,1)S(1)}, bf16[256,1280]{1,0:T(8,128)(2,1)S(1)}, u32[]{:S(2)}, u32[]{:S(2)}) %collective-permute-start.11) | collective-permute-done | bytes 655392 | tf_op jit(solution)/shard_map/ppermute | solution.py:127
  267.0 29.5 %collective-permute-done.9 = bf16[256,1280]{1,0:T(8,128)(2,1)S(1)} collective-permute-done((bf16[256,1280]{1,0:T(8,128)(2,1)S(1)}, bf16[256,1280]{1,0:T(8,128)(2,1)S(1)}, u32[]{:S(2)}, u32[]{:S(2)}) %collective-permute-start.9) | collective-permute-done | bytes 655392 | tf_op jit(solution)/shard_map/ppermute | solution.py:126
  297.6 15.3 %all-to-all-start.2 = ((bf16[32,1,8,1280]{3,2,1,0:T(8,128)(2,1)}), bf16[32,1,8,1280]{3,2,1,0:T(8,128)(2,1)S(1)}, u32[]{:S(2)}, u32[]{:S(2)}) async-start(bf16[32,1,8,1280]{3,2,1,0:T(8,128)(2,1)} %fusion.62), calls=%async_computation.2 | async-start | bytes 1310720 | tf_op jit(solution)/shard_map/all_to_all | solution.py:132
  313.0 3.4 add_convert_fusion
  316.3 9.5 %all-to-all-done.2 = bf16[32,1,8,1280]{3,2,1,0:T(8,128)(2,1)S(1)} async-done(((bf16[32,1,8,1280]{3,2,1,0:T(8,128)(2,1)}), bf16[32,1,8,1280]{3,2,1,0:T(8,128)(2,1)S(1)}, u32[]{:S(2)}, u32[]{:S(2)}) %all-to-all-start.2) | async-done | bytes 655392 | tf_op jit(solution)/shard_map/all_to_all | solution.py:132
  325.8 3.7 %all-to-all-start.4 = ((bf16[32,1,16,1280]{3,2,1,0:T(8,128)(2,1)}), bf16[32,1,16,1280]{3,2,1,0:T(8,128)(2,1)S(1)}, u32[]{:S(2)}, u32[]{:S(2)}) async-start(bf16[32,1,16,1280]{3,2,1,0:T(8,128)(2,1)} %bitcast.30), calls=%async_computation.4 | async-start | bytes 2621440 | tf_op jit(solution)/shard_map/all_to_all | solution.py:132
  330.1 19.2 %all-to-all-done.4 = bf16[32,1,16,1280]{3,2,1,0:T(8,128)(2,1)S(1)} async-done(((bf16[32,1,16,1280]{3,2,1,0:T(8,128)(2,1)}), bf16[32,1,16,1280]{3,2,1,0:T(8,128)(2,1)S(1)}, u32[]{:S(2)}, u32[]{:S(2)}) %all-to-all-start.4) | async-done | bytes 1310752 | tf_op jit(solution)/shard_map/all_to_all | solution.py:132
  349.5 4.4 %fusion.41 = bf16[1,257,1280]{2,1,0:T(8,128)(2,1)} fusion(f32[1,257,1280]{2,1,0:T(8,128)} %copy-done.2, bf16[768,1280]{1,0:T(8,128)(2,1)S(1)} %bitcast.106, f32[257]{0:T(512)S(1)} %get-tuple-element.8, s32[257]{0:T(512)S(1)} %get-tuple-element.6, f32[257]{0:T(512)S(1)} %get-tuple-element.7, s32[257]{0:T(512)S(1)} %get-tuple-element.5), kind=kOutput, calls=%fused_computation.44 | convolution fusion | flops 3033340160 | bytes 3943952 | tf_op jit(solution)/shard_map/dot_general | solution.py:139
  (115 shorter events, 81.5 us)
Async XLA Ops:
  0.0 186.7 %copy-start = (bf16[1,1280,1280]{2,1,0:T(8,128)(2,1)S(1)}, bf16[1,1280,1280]{2,1,0:T(8,128)(2,1)}, u32[]{:S(2)}) copy-start(bf16[1,1280,1280]{2,1,0:T(8,128)(2,1)} %param.16) | copy-start | bytes 9830404
  0.0 8.5 %copy-start.10 = (s32[1,257,2]{1,2,0:T(2,128)S(1)}, s32[1,257,2]{1,2,0:T(2,128)}, u32[]{:S(2)}) copy-start(s32[1,257,2]{1,2,0:T(2,128)} %param.17) | copy-start | bytes 6172
  5.2 18.1 %collective-permute-start.1 = (bf16[1,257,1280]{2,1,0:T(8,128)(2,1)}, bf16[1,257,1280]{2,1,0:T(8,128)(2,1)}, u32[]{:S(2)}, u32[]{:S(2)}) collective-permute-start(bf16[1,257,1280]{2,1,0:T(8,128)(2,1)} %fusion.46), channel_id=1, source_target_pairs={{0,32},{32,64},{64,96},{96,0},{1,33},{33,65},{65,97},{97,1},{2,34}... | collective-permute-start | bytes 1973768 | tf_op jit(solution)/shard_map/ppermute | solution.py:40
  7.2 18.1 %collective-permute-start = (bf16[1,257,1280]{2,1,0:T(8,128)(2,1)}, bf16[1,257,1280]{2,1,0:T(8,128)(2,1)}, u32[]{:S(2)}, u32[]{:S(2)}) collective-permute-start(bf16[1,257,1280]{2,1,0:T(8,128)(2,1)} %fusion.46), channel_id=1, source_target_pairs={{0,96},{32,0},{64,32},{96,64},{1,97},{33,1},{65,33},{97,65},{2,98}... | collective-permute-start | bytes 1973768 | tf_op jit(solution)/shard_map/ppermute | solution.py:41
  25.0 9.4 %collective-permute-start.2 = (bf16[1,257,640]{2,1,0:T(8,128)(2,1)}, bf16[1,257,640]{2,1,0:T(8,128)(2,1)}, u32[]{:S(2)}, u32[]{:S(2)}) collective-permute-start(bf16[1,257,640]{2,1,0:T(8,128)(2,1)} %slice.122), channel_id=1, source_target_pairs={{0,32},{32,64},{64,96},{96,0},{1,33},{33,65},{65,97},{97,1},{2,34}... | collective-permute-start | bytes 986888 | tf_op jit(solution)/shard_map/ppermute | solution.py:44
  27.0 8.1 %collective-permute-start.3 = (bf16[1,257,640]{2,1,0:T(8,128)(2,1)}, bf16[1,257,640]{2,1,0:T(8,128)(2,1)}, u32[]{:S(2)}, u32[]{:S(2)}) collective-permute-start(bf16[1,257,640]{2,1,0:T(8,128)(2,1)} %slice.123), channel_id=1, source_target_pairs={{0,96},{32,0},{64,32},{96,64},{1,97},{33,1},{65,33},{97,65},{2,98}... | collective-permute-start | bytes 986888 | tf_op jit(solution)/shard_map/ppermute | solution.py:45
  71.6 14.2 %all-to-all-start = ((bf16[4,257,320]{2,1,0:T(8,128)(2,1)}), bf16[4,257,320]{2,1,0:T(8,128)(2,1)}, u32[]{:S(2)}, u32[]{:S(2)}) async-start(bf16[4,257,320]{2,1,0:T(8,128)(2,1)} %fusion.57), calls=%async_computation | async-start | bytes 1622016 | tf_op jit(solution)/shard_map/all_to_all | solution.py:71
  94.9 25.7 %all-to-all-start.1 = ((bf16[32,1,8,1280]{3,2,1,0:T(8,128)(2,1)}), bf16[32,1,8,1280]{3,2,1,0:T(8,128)(2,1)}, u32[]{:S(2)}, u32[]{:S(2)}) async-start(bf16[32,1,8,1280]{3,2,1,0:T(8,128)(2,1)} %slice.131), calls=%async_computation.1 | async-start | bytes 1310720 | tf_op jit(solution)/shard_map/all_to_all | solution.py:102
  120.6 24.1 %all-to-all-start.3 = ((bf16[32,1,16,1280]{3,2,1,0:T(8,128)(2,1)}), bf16[32,1,16,1280]{3,2,1,0:T(8,128)(2,1)}, u32[]{:S(2)}, u32[]{:S(2)}) async-start(bf16[32,1,16,1280]{3,2,1,0:T(8,128)(2,1)} %slice.140), calls=%async_computation.3 | async-start | bytes 2621440 | tf_op jit(solution)/shard_map/all_to_all | solution.py:102
  125.0 22.3 %collective-permute-start.5 = (bf16[256,1280]{1,0:T(8,128)(2,1)}, bf16[256,1280]{1,0:T(8,128)(2,1)}, u32[]{:S(2)}, u32[]{:S(2)}) collective-permute-start(bf16[256,1280]{1,0:T(8,128)(2,1)} %bitcast.22), channel_id=1, source_target_pairs={{0,32},{32,64},{64,96},{96,0},{1,33},{33,65},{65,97},{97,1},{2,34}... | collective-permute-start | bytes 1966088 | tf_op jit(solution)/shard_map/ppermute | solution.py:104
  125.7 25.2 %collective-permute-start.4 = (bf16[256,1280]{1,0:T(8,128)(2,1)}, bf16[256,1280]{1,0:T(8,128)(2,1)}, u32[]{:S(2)}, u32[]{:S(2)}) collective-permute-start(bf16[256,1280]{1,0:T(8,128)(2,1)} %bitcast.22), channel_id=1, source_target_pairs={{0,96},{32,0},{64,32},{96,64},{1,97},{33,1},{65,33},{97,65},{2,98}... | collective-permute-start | bytes 1966088 | tf_op jit(solution)/shard_map/ppermute | solution.py:105
  144.6 52.9 %collective-permute-start.13 = (bf16[512,1280]{1,0:T(8,128)(2,1)}, bf16[512,1280]{1,0:T(8,128)(2,1)}, u32[]{:S(2)}, u32[]{:S(2)}) collective-permute-start(bf16[512,1280]{1,0:T(8,128)(2,1)} %bitcast.28), channel_id=1, source_target_pairs={{0,32},{32,64},{64,96},{96,0},{1,33},{33,65},{65,97},{97,1},{2,34}... | collective-permute-start | bytes 3932168 | tf_op jit(solution)/shard_map/ppermute | solution.py:104
  145.2 53.6 %collective-permute-start.12 = (bf16[512,1280]{1,0:T(8,128)(2,1)}, bf16[512,1280]{1,0:T(8,128)(2,1)}, u32[]{:S(2)}, u32[]{:S(2)}) collective-permute-start(bf16[512,1280]{1,0:T(8,128)(2,1)} %bitcast.28), channel_id=1, source_target_pairs={{0,96},{32,0},{64,32},{96,64},{1,97},{33,1},{65,33},{97,65},{2,98}... | collective-permute-start | bytes 3932168 | tf_op jit(solution)/shard_map/ppermute | solution.py:105
  148.3 34.9 %collective-permute-start.6 = (bf16[128,1280]{1,0:T(8,128)(2,1)S(1)}, bf16[128,1280]{1,0:T(8,128)(2,1)S(1)}, u32[]{:S(2)}, u32[]{:S(2)}) collective-permute-start(bf16[128,1280]{1,0:T(8,128)(2,1)S(1)} %slice.132), channel_id=1, source_target_pairs={{0,32},{32,64},{64,96},{96,0},{1,33},{33,65},{65,97},{97,1},{2,34}... | collective-permute-start | bytes 983048 | tf_op jit(solution)/shard_map/ppermute | solution.py:108
  151.9 32.1 %collective-permute-start.7 = (bf16[128,1280]{1,0:T(8,128)(2,1)S(1)}, bf16[128,1280]{1,0:T(8,128)(2,1)S(1)}, u32[]{:S(2)}, u32[]{:S(2)}) collective-permute-start(bf16[128,1280]{1,0:T(8,128)(2,1)S(1)} %slice.133), channel_id=1, source_target_pairs={{0,96},{32,0},{64,32},{96,64},{1,97},{33,1},{65,33},{97,65},{2,98}... | collective-permute-start | bytes 983048 | tf_op jit(solution)/shard_map/ppermute | solution.py:109
  198.7 16.5 %collective-permute-start.14 = (bf16[256,1280]{1,0:T(8,128)(2,1)S(1)}, bf16[256,1280]{1,0:T(8,128)(2,1)S(1)}, u32[]{:S(2)}, u32[]{:S(2)}) collective-permute-start(bf16[256,1280]{1,0:T(8,128)(2,1)S(1)} %slice.141), channel_id=1, source_target_pairs={{0,32},{32,64},{64,96},{96,0},{1,33},{33,65},{65,97},{97,1},{2,34}... | collective-permute-start | bytes 1966088 | tf_op jit(solution)/shard_map/ppermute | solution.py:108
  199.9 16.2 %collective-permute-start.15 = (bf16[256,1280]{1,0:T(8,128)(2,1)S(1)}, bf16[256,1280]{1,0:T(8,128)(2,1)S(1)}, u32[]{:S(2)}, u32[]{:S(2)}) collective-permute-start(bf16[256,1280]{1,0:T(8,128)(2,1)S(1)} %slice.142), channel_id=1, source_target_pairs={{0,96},{32,0},{64,32},{96,64},{1,97},{33,1},{65,33},{97,65},{2,98}... | collective-permute-start | bytes 1966088 | tf_op jit(solution)/shard_map/ppermute | solution.py:109
  205.0 37.9 %collective-permute-start.8 = (bf16[128,1280]{1,0:T(8,128)(2,1)}, bf16[128,1280]{1,0:T(8,128)(2,1)}, u32[]{:S(2)}, u32[]{:S(2)}) collective-permute-start(bf16[128,1280]{1,0:T(8,128)(2,1)} %get-tuple-element.17), channel_id=1, source_target_pairs={{0,32},{32,64},{64,96},{96,0},{1,33},{33,65},{65,97},{97,1},{2,34}... | collective-permute-start | bytes 983048 | tf_op jit(solution)/shard_map/ppermute | solution.py:118
  205.0 37.9 %collective-permute-start.10 = (bf16[128,1280]{1,0:T(8,128)(2,1)}, bf16[128,1280]{1,0:T(8,128)(2,1)}, u32[]{:S(2)}, u32[]{:S(2)}) collective-permute-start(bf16[128,1280]{1,0:T(8,128)(2,1)} %get-tuple-element.18), channel_id=1, source_target_pairs={{0,96},{32,0},{64,32},{96,64},{1,97},{33,1},{65,33},{97,65},{2,98}... | collective-permute-start | bytes 983048 | tf_op jit(solution)/shard_map/ppermute | solution.py:119
  238.0 4.9 %copy-start.5 = (bf16[1024,1280]{1,0:T(8,128)(2,1)S(1)}, bf16[1024,1280]{1,0:T(8,128)(2,1)}, u32[]{:S(2)}) copy-start(bf16[1024,1280]{1,0:T(8,128)(2,1)} %convolution_convert_fusion.1) | copy-start | bytes 7864324
  238.0 6.1 %copy-start.8 = (bf16[128,1280]{1,0:T(8,128)(2,1)S(1)}, bf16[128,1280]{1,0:T(8,128)(2,1)}, u32[]{:S(2)}) copy-start(bf16[128,1280]{1,0:T(8,128)(2,1)} %get-tuple-element.19) | copy-start | bytes 983044
  240.0 13.9 %collective-permute-start.16 = (bf16[256,1280]{1,0:T(8,128)(2,1)S(1)}, bf16[256,1280]{1,0:T(8,128)(2,1)S(1)}, u32[]{:S(2)}, u32[]{:S(2)}) collective-permute-start(bf16[256,1280]{1,0:T(8,128)(2,1)S(1)} %get-tuple-element.11), channel_id=1, source_target_pairs={{0,32},{32,64},{64,96},{96,0},{1,33},{33,65},{65,97},{97,1},{2,34}... | collective-permute-start | bytes 1966088 | tf_op jit(solution)/shard_map/ppermute | solution.py:118
  240.1 13.8 %collective-permute-start.18 = (bf16[256,1280]{1,0:T(8,128)(2,1)S(1)}, bf16[256,1280]{1,0:T(8,128)(2,1)S(1)}, u32[]{:S(2)}, u32[]{:S(2)}) collective-permute-start(bf16[256,1280]{1,0:T(8,128)(2,1)S(1)} %get-tuple-element.12), channel_id=1, source_target_pairs={{0,96},{32,0},{64,32},{96,64},{1,97},{33,1},{65,33},{97,65},{2,98}... | collective-permute-start | bytes 1966088 | tf_op jit(solution)/shard_map/ppermute | solution.py:119
  244.2 22.8 %collective-permute-start.11 = (bf16[256,1280]{1,0:T(8,128)(2,1)S(1)}, bf16[256,1280]{1,0:T(8,128)(2,1)S(1)}, u32[]{:S(2)}, u32[]{:S(2)}) collective-permute-start(bf16[256,1280]{1,0:T(8,128)(2,1)S(1)} %pad_maximum_fusion.5), channel_id=1, source_target_pairs={{0,96},{32,0},{64,32},{96,64},{1,97},{33,1},{65,33},{97,65},{2,98}... | collective-permute-start | bytes 1966088 | tf_op jit(solution)/shard_map/ppermute | solution.py:127
  255.5 4.8 %copy-start.7 = (bf16[128,1280]{1,0:T(8,128)(2,1)S(1)}, bf16[128,1280]{1,0:T(8,128)(2,1)}, u32[]{:S(2)}) copy-start(bf16[128,1280]{1,0:T(8,128)(2,1)} %get-tuple-element.20) | copy-start | bytes 983044
  256.7 56.2 %collective-permute-start.19 = (bf16[512,1280]{1,0:T(8,128)(2,1)}, bf16[512,1280]{1,0:T(8,128)(2,1)}, u32[]{:S(2)}, u32[]{:S(2)}) collective-permute-start(bf16[512,1280]{1,0:T(8,128)(2,1)} %pad_maximum_fusion.3), channel_id=1, source_target_pairs={{0,96},{32,0},{64,32},{96,64},{1,97},{33,1},{65,33},{97,65},{2,98}... | collective-permute-start | bytes 3932168 | tf_op jit(solution)/shard_map/ppermute | solution.py:127
  260.3 52.6 %collective-permute-start.17 = (bf16[512,1280]{1,0:T(8,128)(2,1)}, bf16[512,1280]{1,0:T(8,128)(2,1)S(1)}, u32[]{:S(2)}, u32[]{:S(2)}) collective-permute-start(bf16[512,1280]{1,0:T(8,128)(2,1)} %pad_maximum_fusion.2), channel_id=1, source_target_pairs={{0,32},{32,64},{64,96},{96,0},{1,33},{33,65},{65,97},{97,1},{2,34}... | collective-permute-start | bytes 3932168 | tf_op jit(solution)/shard_map/ppermute | solution.py:126
  260.4 36.1 %collective-permute-start.9 = (bf16[256,1280]{1,0:T(8,128)(2,1)S(1)}, bf16[256,1280]{1,0:T(8,128)(2,1)S(1)}, u32[]{:S(2)}, u32[]{:S(2)}) collective-permute-start(bf16[256,1280]{1,0:T(8,128)(2,1)S(1)} %pad_maximum_fusion.4), channel_id=1, source_target_pairs={{0,32},{32,64},{64,96},{96,0},{1,33},{33,65},{65,97},{97,1},{2,34}... | collective-permute-start | bytes 1966088 | tf_op jit(solution)/shard_map/ppermute | solution.py:126
  297.6 28.2 %all-to-all-start.2 = ((bf16[32,1,8,1280]{3,2,1,0:T(8,128)(2,1)}), bf16[32,1,8,1280]{3,2,1,0:T(8,128)(2,1)S(1)}, u32[]{:S(2)}, u32[]{:S(2)}) async-start(bf16[32,1,8,1280]{3,2,1,0:T(8,128)(2,1)} %fusion.62), calls=%async_computation.2 | async-start | bytes 1310720 | tf_op jit(solution)/shard_map/all_to_all | solution.py:132
  312.9 16.7 %copy-start.4 = (bf16[257,1280]{1,0:T(8,128)(2,1)S(1)}, bf16[257,1280]{1,0:T(8,128)(2,1)}, u32[]{:S(2)}) copy-start(bf16[257,1280]{1,0:T(8,128)(2,1)} %copy-done.3) | copy-start | bytes 1973764
  312.9 16.7 %copy-start.9 = (bf16[1280,32]{0,1:T(8,128)(2,1)S(1)}, bf16[1280,32]{0,1:T(8,128)(2,1)}, u32[]{:S(2)}) copy-start(bf16[1280,32]{0,1:T(8,128)(2,1)} %param.14) | copy-start | bytes 245764
  325.8 23.5 %all-to-all-start.4 = ((bf16[32,1,16,1280]{3,2,1,0:T(8,128)(2,1)}), bf16[32,1,16,1280]{3,2,1,0:T(8,128)(2,1)S(1)}, u32[]{:S(2)}, u32[]{:S(2)}) async-start(bf16[32,1,16,1280]{3,2,1,0:T(8,128)(2,1)} %bitcast.30), calls=%async_computation.4 | async-start | bytes 2621440 | tf_op jit(solution)/shard_map/all_to_all | solution.py:132
  (4 other events, 7.6 us)
where the time goes:
time: 355 us; the launch traced here: 354 us
  waiting for transfers between devices  152 us (43%)
  starting transfers between devices  67.4 us (19%)
  matrix products  64 us (18%)
  local copies, waits for them, and re-layouts  48.1 us (14%)
  other arithmetic  22.1 us (6%)
    ppermute x2, waiting for transfers between devices, shards(): lax.ppermute(came_behind[:half], 'node', ahead)  31.6 us
    ppermute x2, waiting for transfers between devices, shards(): back_behind = lax.ppermute(to_next.astype(jnp.bfloat16), 'node', ahead)  29.5 us
    dot_general x2, matrix products, shards(): jnp.dot(hidden, w_out[0], preferred_element_type=jnp.float32)  29.5 us
    all_to_all x2, waiting for transfers between devices, shards(): lax.all_to_all(summed, 'ep', split_axis=0, concat_axis=0, tiled=True)  28.7 us
    all_to_all x2, waiting for transfers between devices, shards(): lax.all_to_all(sent, 'ep', split_axis=0, concat_axis=0, tiled=True)  25.3 us
    all_to_all x2, starting transfers between devices, shards(): lax.all_to_all(summed, 'ep', split_axis=0, concat_axis=0, tiled=True)  19 us
    all_to_all x2, starting transfers between devices, shards(): lax.all_to_all(sent, 'ep', split_axis=0, concat_axis=0, tiled=True)  17.2 us
    unnamed x31, local copies, waits for them, and re-layouts  15.3 us
  transfers between devices with their start and end apart: 25, of which 13 were waited for; matrix products, arithmetic and copies ran while one was open for 22% of the time, Pallas kernels for 0%

commit v1 on v0

--- a/solution.py
+++ b/solution.py
@@ -94,7 +94,7 @@
         hits.astype(jnp.bfloat16), token_rows, preferred_element_type=jnp.float32
     ).astype(jnp.bfloat16)
     outgoing = gathered.reshape(column_count, local_experts, slot_count, width)
-    bounds = [0, slot_count // 3, slot_count]
+    bounds = [0, 2 * slot_count // 3, slot_count]
     pieces = []
     for low, high in zip(bounds[:-1], bounds[1:]):
         chunk = high - low

time: 355 us -> 356 us (level)
  no operation moved by 1% of the time
where the time goes in v1:
time: 356 us; the launch traced here: 354 us
  waiting for transfers between devices  152 us (43%)
  starting transfers between devices  67.4 us (19%)
  matrix products  64 us (18%)
  local copies, waits for them, and re-layouts  48.1 us (14%)
  other arithmetic  22.1 us (6%)
    ppermute x2, waiting for transfers between devices, shards(): lax.ppermute(came_behind[:half], 'node', ahead)  31.6 us
    ppermute x2, waiting for transfers between devices, shards(): back_behind = lax.ppermute(to_next.astype(jnp.bfloat16), 'node', ahead)  29.5 us
    dot_general x2, matrix products, shards(): jnp.dot(hidden, w_out[0], preferred_element_type=jnp.float32)  29.5 us
    all_to_all x2, waiting for transfers between devices, shards(): lax.all_to_all(summed, 'ep', split_axis=0, concat_axis=0, tiled=True)  28.7 us
    all_to_all x2, waiting for transfers between devices, shards(): lax.all_to_all(sent, 'ep', split_axis=0, concat_axis=0, tiled=True)  25.3 us
    all_to_all x2, starting transfers between devices, shards(): lax.all_to_all(summed, 'ep', split_axis=0, concat_axis=0, tiled=True)  19 us
    all_to_all x2, starting transfers between devices, shards(): lax.all_to_all(sent, 'ep', split_axis=0, concat_axis=0, tiled=True)  17.2 us
    unnamed x31, local copies, waits for them, and re-layouts  15.3 us
  transfers between devices with their start and end apart: 25, of which 13 were waited for; matrix products, arithmetic and copies ran while one was open for 22% of the time, Pallas kernels for 0%

profile of v1, /device:TPU:1, one launch (start us, length us, event | category | flops | bytes accessed | tf_op | source)
XLA Modules:
  0.0 353.9 jit_solution(170326908689706974)
XLA Ops:
  9.4 3.0 reduce-window.6
  12.4 10.9 %collective-permute-done.1 = bf16[1,257,1280]{2,1,0:T(8,128)(2,1)} collective-permute-done((bf16[1,257,1280]{2,1,0:T(8,128)(2,1)}, bf16[1,257,1280]{2,1,0:T(8,128)(2,1)}, u32[]{:S(2)}, u32[]{:S(2)}) %collective-permute-start.1) | collective-permute-done | bytes 657952 | tf_op jit(solution)/shard_map/ppermute | solution.py:40
  35.1 4.5 %fusion.48 = bf16[4,320,257]{1,2,0:T(8,128)(2,1)} fusion(bf16[1280,320]{0,1:T(8,128)(2,1)} %param.10, bf16[1,257,1280]{2,1,0:T(8,128)(2,1)} %collective-permute-done.1, bf16[1,257,640]{2,1,0:T(8,128)(2,1)} %collective-permute-done.3, bf16[1,257,640]{2,1,0:T(8,128)(2,1)} %collective-permute-done.2, bf16[1,257,1280]{2,1,0:T(8,128)(2,1)} %collective-permute-done, ...), kind=kOutput, calls=%fused_computation.66 | convolution fusion | flops 855624960 | bytes 4108800 | tf_op jit(solution)/shard_map/ctd,de->cet/dot_general | solution.py:51
  41.9 4.5 %fusion.47 = bf16[4,320,257]{1,2,0:T(8,128)(2,1)} fusion(bf16[1280,320]{0,1:T(8,128)(2,1)} %param.12, bf16[1,257,1280]{2,1,0:T(8,128)(2,1)} %collective-permute-done.1, bf16[1,257,640]{2,1,0:T(8,128)(2,1)} %collective-permute-done.3, bf16[1,257,640]{2,1,0:T(8,128)(2,1)} %collective-permute-done.2, bf16[1,257,1280]{2,1,0:T(8,128)(2,1)} %collective-permute-done, ...), kind=kOutput, calls=%fused_computation.65 | convolution fusion | flops 855624960 | bytes 4108800 | tf_op jit(solution)/shard_map/ctd,de->cet/dot_general | solution.py:57
  48.6 4.5 %fusion.49 = bf16[4,320,257]{1,2,0:T(8,128)(2,1)} fusion(bf16[1280,320]{0,1:T(8,128)(2,1)} %param.11, bf16[1,257,1280]{2,1,0:T(8,128)(2,1)} %collective-permute-done.1, bf16[1,257,640]{2,1,0:T(8,128)(2,1)} %collective-permute-done.3, bf16[1,257,640]{2,1,0:T(8,128)(2,1)} %collective-permute-done.2, bf16[1,257,1280]{2,1,0:T(8,128)(2,1)} %collective-permute-done, ...), kind=kOutput, calls=%fused_computation.67 | convolution fusion | flops 855624960 | bytes 4108800 | tf_op jit(solution)/shard_map/ctd,de->cet/dot_general | solution.py:54
  55.3 6.5 %fusion.87 = (f32[4,4,257]{2,1,0:T(4,128)S(1)}, f32[4,4,257,257]{2,3,1,0:T(8,128)}) fusion(bf16[4,4,80,257]{3,2,1,0:T(8,128)(2,1)} %bitcast.108, bf16[4,4,80,257]{3,2,1,0:T(8,128)(2,1)} %bitcast.109), kind=kOutput, calls=%fused_computation.138 | convolution fusion | flops 172256048 | bytes 5559424 | tf_op jit(solution)/shard_map/sub | solution.py:66
  61.8 5.1 %fusion.44 = bf16[4,4,80,257]{3,2,1,0:T(8,128)(2,1)} fusion(bf16[4,4,80,257]{3,2,1,0:T(8,128)(2,1)} %bitcast.107, f32[4,4,257,257]{2,3,1,0:T(8,128)} %get-tuple-element.22, f32[4,4,257]{2,1,0:T(4,128)S(1)} %get-tuple-element.21), kind=kOutput, calls=%fused_computation.52 | convolution fusion | flops 171527968 | bytes 5559424 | tf_op jit(solution)/shard_map/chqk,chdk->cqhd/dot_general | solution.py:67
  71.6 4.6 %all-to-all-start = ((bf16[4,257,320]{2,1,0:T(8,128)(2,1)}), bf16[4,257,320]{2,1,0:T(8,128)(2,1)}, u32[]{:S(2)}, u32[]{:S(2)}) async-start(bf16[4,257,320]{2,1,0:T(8,128)(2,1)} %fusion.57), calls=%async_computation | async-start | bytes 1622016 | tf_op jit(solution)/shard_map/all_to_all | solution.py:71
  77.6 8.2 %all-to-all-done = bf16[4,257,320]{2,1,0:T(8,128)(2,1)} async-done(((bf16[4,257,320]{2,1,0:T(8,128)(2,1)}), bf16[4,257,320]{2,1,0:T(8,128)(2,1)}, u32[]{:S(2)}, u32[]{:S(2)}) %all-to-all-start) | async-done | bytes 657952 | tf_op jit(solution)/shard_map/all_to_all | solution.py:71
  85.7 3.6 %fusion.88 = (f32[257]{0:T(512)S(1)}, f32[1,257,1280]{2,1,0:T(8,128)S(1)}) fusion(bf16[4,257,320]{2,1,0:T(8,128)(2,1)} %all-to-all-done, bf16[4,320,1280]{2,1,0:T(8,128)(2,1)} %bitcast.112, bf16[1,257,1280]{2,1,0:T(8,128)(2,1)} %param.9), kind=kOutput, calls=%fused_computation.139 | convolution fusion | flops 843124224 | bytes 5909508 | tf_op jit(solution)/shard_map/gtd,gde->te/dot_general | solution.py:72
  94.9 12.7 %all-to-all-start.3 = ((bf16[32,1,8,1280]{3,2,1,0:T(8,128)(2,1)}), bf16[32,1,8,1280]{3,2,1,0:T(8,128)(2,1)}, u32[]{:S(2)}, u32[]{:S(2)}) async-start(bf16[32,1,8,1280]{3,2,1,0:T(8,128)(2,1)} %slice.140), calls=%async_computation.3 | async-start | bytes 1310720 | tf_op jit(solution)/shard_map/all_to_all | solution.py:102
  107.6 2.5 slice.131
  110.1 10.5 %all-to-all-done.3 = bf16[32,1,8,1280]{3,2,1,0:T(8,128)(2,1)} async-done(((bf16[32,1,8,1280]{3,2,1,0:T(8,128)(2,1)}), bf16[32,1,8,1280]{3,2,1,0:T(8,128)(2,1)}, u32[]{:S(2)}, u32[]{:S(2)}) %all-to-all-start.3) | async-done | bytes 655392 | tf_op jit(solution)/shard_map/all_to_all | solution.py:102
  120.6 4.5 %all-to-all-start.1 = ((bf16[32,1,16,1280]{3,2,1,0:T(8,128)(2,1)}), bf16[32,1,16,1280]{3,2,1,0:T(8,128)(2,1)}, u32[]{:S(2)}, u32[]{:S(2)}) async-start(bf16[32,1,16,1280]{3,2,1,0:T(8,128)(2,1)} %slice.131), calls=%async_computation.1 | async-start | bytes 2621440 | tf_op jit(solution)/shard_map/all_to_all | solution.py:102
  129.8 14.8 %all-to-all-done.1 = bf16[32,1,16,1280]{3,2,1,0:T(8,128)(2,1)} async-done(((bf16[32,1,16,1280]{3,2,1,0:T(8,128)(2,1)}), bf16[32,1,16,1280]{3,2,1,0:T(8,128)(2,1)}, u32[]{:S(2)}, u32[]{:S(2)}) %all-to-all-start.1) | async-done | bytes 1310752 | tf_op jit(solution)/shard_map/all_to_all | solution.py:102
  151.9 2.7 collective-permute-start.15
  156.6 26.6 %collective-permute-done.14 = bf16[128,1280]{1,0:T(8,128)(2,1)S(1)} collective-permute-done((bf16[128,1280]{1,0:T(8,128)(2,1)S(1)}, bf16[128,1280]{1,0:T(8,128)(2,1)S(1)}, u32[]{:S(2)}, u32[]{:S(2)}) %collective-permute-start.14) | collective-permute-done | bytes 327712 | tf_op jit(solution)/shard_map/ppermute | solution.py:108
  186.7 10.9 %convolution_convert_fusion.1 = bf16[1024,1280]{1,0:T(8,128)(2,1)} fusion(bf16[1,1280,1280]{2,1,0:T(8,128)(2,1)S(1)} %copy-done, bf16[1024,1280]{1,0:T(8,128)(2,1)} %constant_dynamic-update-slice_fusion.5, bf16[1,1280,1280]{2,1,0:T(8,128)(2,1)} %param.15), kind=kOutput, calls=%fused_computation.28 | convolution fusion | flops 6723993600 | bytes 11796480 | tf_op jit(solution)/shard_map/dot_general | solution.py:116
  199.9 2.7 collective-permute-start.7
  205.0 2.7 collective-permute-start.18
  210.2 5.0 %collective-permute-done.6 = bf16[256,1280]{1,0:T(8,128)(2,1)S(1)} collective-permute-done((bf16[256,1280]{1,0:T(8,128)(2,1)S(1)}, bf16[256,1280]{1,0:T(8,128)(2,1)S(1)}, u32[]{:S(2)}, u32[]{:S(2)}) %collective-permute-start.6) | collective-permute-done | bytes 655392 | tf_op jit(solution)/shard_map/ppermute | solution.py:108
  219.4 18.6 %convolution_convert_fusion = bf16[2048,1280]{1,0:T(8,128)(2,1)} fusion(bf16[1,1280,1280]{2,1,0:T(8,128)(2,1)S(1)} %copy-done, bf16[2048,1280]{1,0:T(8,128)(2,1)} %constant_dynamic-update-slice_fusion, bf16[1,1280,1280]{2,1,0:T(8,128)(2,1)} %param.15), kind=kOutput, calls=%fused_computation.11 | convolution fusion | flops 13447987200 | bytes 17039360 | tf_op jit(solution)/shard_map/dot_general | solution.py:116
  240.1 2.8 collective-permute-start.10
  245.7 8.2 %collective-permute-done.8 = bf16[256,1280]{1,0:T(8,128)(2,1)S(1)} collective-permute-done((bf16[256,1280]{1,0:T(8,128)(2,1)S(1)}, bf16[256,1280]{1,0:T(8,128)(2,1)S(1)}, u32[]{:S(2)}, u32[]{:S(2)}) %collective-permute-start.8) | collective-permute-done | bytes 655392 | tf_op jit(solution)/shard_map/ppermute | solution.py:118
  260.5 6.5 %collective-permute-done.19 = bf16[256,1280]{1,0:T(8,128)(2,1)S(1)} collective-permute-done((bf16[256,1280]{1,0:T(8,128)(2,1)S(1)}, bf16[256,1280]{1,0:T(8,128)(2,1)S(1)}, u32[]{:S(2)}, u32[]{:S(2)}) %collective-permute-start.19) | collective-permute-done | bytes 655392 | tf_op jit(solution)/shard_map/ppermute | solution.py:127
  267.0 29.5 %collective-permute-done.17 = bf16[256,1280]{1,0:T(8,128)(2,1)S(1)} collective-permute-done((bf16[256,1280]{1,0:T(8,128)(2,1)S(1)}, bf16[256,1280]{1,0:T(8,128)(2,1)S(1)}, u32[]{:S(2)}, u32[]{:S(2)}) %collective-permute-start.17) | collective-permute-done | bytes 655392 | tf_op jit(solution)/shard_map/ppermute | solution.py:126
  297.6 15.3 %all-to-all-start.4 = ((bf16[32,1,8,1280]{3,2,1,0:T(8,128)(2,1)}), bf16[32,1,8,1280]{3,2,1,0:T(8,128)(2,1)S(1)}, u32[]{:S(2)}, u32[]{:S(2)}) async-start(bf16[32,1,8,1280]{3,2,1,0:T(8,128)(2,1)} %fusion.62), calls=%async_computation.4 | async-start | bytes 1310720 | tf_op jit(solution)/shard_map/all_to_all | solution.py:132
  313.0 3.4 add_convert_fusion
  316.3 9.5 %all-to-all-done.4 = bf16[32,1,8,1280]{3,2,1,0:T(8,128)(2,1)S(1)} async-done(((bf16[32,1,8,1280]{3,2,1,0:T(8,128)(2,1)}), bf16[32,1,8,1280]{3,2,1,0:T(8,128)(2,1)S(1)}, u32[]{:S(2)}, u32[]{:S(2)}) %all-to-all-start.4) | async-done | bytes 655392 | tf_op jit(solution)/shard_map/all_to_all | solution.py:132
  325.8 3.7 %all-to-all-start.2 = ((bf16[32,1,16,1280]{3,2,1,0:T(8,128)(2,1)}), bf16[32,1,16,1280]{3,2,1,0:T(8,128)(2,1)S(1)}, u32[]{:S(2)}, u32[]{:S(2)}) async-start(bf16[32,1,16,1280]{3,2,1,0:T(8,128)(2,1)} %bitcast.26), calls=%async_computation.2 | async-start | bytes 2621440 | tf_op jit(solution)/shard_map/all_to_all | solution.py:132
  330.1 19.2 %all-to-all-done.2 = bf16[32,1,16,1280]{3,2,1,0:T(8,128)(2,1)S(1)} async-done(((bf16[32,1,16,1280]{3,2,1,0:T(8,128)(2,1)}), bf16[32,1,16,1280]{3,2,1,0:T(8,128)(2,1)S(1)}, u32[]{:S(2)}, u32[]{:S(2)}) %all-to-all-start.2) | async-done | bytes 1310752 | tf_op jit(solution)/shard_map/all_to_all | solution.py:132
  349.5 4.4 %fusion.41 = bf16[1,257,1280]{2,1,0:T(8,128)(2,1)} fusion(f32[1,257,1280]{2,1,0:T(8,128)} %copy-done.2, bf16[768,1280]{1,0:T(8,128)(2,1)S(1)} %bitcast.106, f32[257]{0:T(512)S(1)} %get-tuple-element.8, s32[257]{0:T(512)S(1)} %get-tuple-element.6, f32[257]{0:T(512)S(1)} %get-tuple-element.7, s32[257]{0:T(512)S(1)} %get-tuple-element.5), kind=kOutput, calls=%fused_computation.44 | convolution fusion | flops 3033340160 | bytes 3943952 | tf_op jit(solution)/shard_map/dot_general | solution.py:139
  (115 shorter events, 81.5 us)
Async XLA Ops:
  0.0 186.7 %copy-start = (bf16[1,1280,1280]{2,1,0:T(8,128)(2,1)S(1)}, bf16[1,1280,1280]{2,1,0:T(8,128)(2,1)}, u32[]{:S(2)}) copy-start(bf16[1,1280,1280]{2,1,0:T(8,128)(2,1)} %param.16) | copy-start | bytes 9830404
  0.0 8.5 %copy-start.10 = (s32[1,257,2]{1,2,0:T(2,128)S(1)}, s32[1,257,2]{1,2,0:T(2,128)}, u32[]{:S(2)}) copy-start(s32[1,257,2]{1,2,0:T(2,128)} %param.17) | copy-start | bytes 6172
  5.2 18.1 %collective-permute-start.1 = (bf16[1,257,1280]{2,1,0:T(8,128)(2,1)}, bf16[1,257,1280]{2,1,0:T(8,128)(2,1)}, u32[]{:S(2)}, u32[]{:S(2)}) collective-permute-start(bf16[1,257,1280]{2,1,0:T(8,128)(2,1)} %fusion.46), channel_id=1, source_target_pairs={{0,32},{32,64},{64,96},{96,0},{1,33},{33,65},{65,97},{97,1},{2,34}... | collective-permute-start | bytes 1973768 | tf_op jit(solution)/shard_map/ppermute | solution.py:40
  7.2 18.1 %collective-permute-start = (bf16[1,257,1280]{2,1,0:T(8,128)(2,1)}, bf16[1,257,1280]{2,1,0:T(8,128)(2,1)}, u32[]{:S(2)}, u32[]{:S(2)}) collective-permute-start(bf16[1,257,1280]{2,1,0:T(8,128)(2,1)} %fusion.46), channel_id=1, source_target_pairs={{0,96},{32,0},{64,32},{96,64},{1,97},{33,1},{65,33},{97,65},{2,98}... | collective-permute-start | bytes 1973768 | tf_op jit(solution)/shard_map/ppermute | solution.py:41
  25.0 9.4 %collective-permute-start.2 = (bf16[1,257,640]{2,1,0:T(8,128)(2,1)}, bf16[1,257,640]{2,1,0:T(8,128)(2,1)}, u32[]{:S(2)}, u32[]{:S(2)}) collective-permute-start(bf16[1,257,640]{2,1,0:T(8,128)(2,1)} %slice.122), channel_id=1, source_target_pairs={{0,32},{32,64},{64,96},{96,0},{1,33},{33,65},{65,97},{97,1},{2,34}... | collective-permute-start | bytes 986888 | tf_op jit(solution)/shard_map/ppermute | solution.py:44
  27.0 8.1 %collective-permute-start.3 = (bf16[1,257,640]{2,1,0:T(8,128)(2,1)}, bf16[1,257,640]{2,1,0:T(8,128)(2,1)}, u32[]{:S(2)}, u32[]{:S(2)}) collective-permute-start(bf16[1,257,640]{2,1,0:T(8,128)(2,1)} %slice.123), channel_id=1, source_target_pairs={{0,96},{32,0},{64,32},{96,64},{1,97},{33,1},{65,33},{97,65},{2,98}... | collective-permute-start | bytes 986888 | tf_op jit(solution)/shard_map/ppermute | solution.py:45
  71.6 14.2 %all-to-all-start = ((bf16[4,257,320]{2,1,0:T(8,128)(2,1)}), bf16[4,257,320]{2,1,0:T(8,128)(2,1)}, u32[]{:S(2)}, u32[]{:S(2)}) async-start(bf16[4,257,320]{2,1,0:T(8,128)(2,1)} %fusion.57), calls=%async_computation | async-start | bytes 1622016 | tf_op jit(solution)/shard_map/all_to_all | solution.py:71
  94.9 25.7 %all-to-all-start.3 = ((bf16[32,1,8,1280]{3,2,1,0:T(8,128)(2,1)}), bf16[32,1,8,1280]{3,2,1,0:T(8,128)(2,1)}, u32[]{:S(2)}, u32[]{:S(2)}) async-start(bf16[32,1,8,1280]{3,2,1,0:T(8,128)(2,1)} %slice.140), calls=%async_computation.3 | async-start | bytes 1310720 | tf_op jit(solution)/shard_map/all_to_all | solution.py:102
  120.6 24.1 %all-to-all-start.1 = ((bf16[32,1,16,1280]{3,2,1,0:T(8,128)(2,1)}), bf16[32,1,16,1280]{3,2,1,0:T(8,128)(2,1)}, u32[]{:S(2)}, u32[]{:S(2)}) async-start(bf16[32,1,16,1280]{3,2,1,0:T(8,128)(2,1)} %slice.131), calls=%async_computation.1 | async-start | bytes 2621440 | tf_op jit(solution)/shard_map/all_to_all | solution.py:102
  125.0 22.3 %collective-permute-start.13 = (bf16[256,1280]{1,0:T(8,128)(2,1)}, bf16[256,1280]{1,0:T(8,128)(2,1)}, u32[]{:S(2)}, u32[]{:S(2)}) collective-permute-start(bf16[256,1280]{1,0:T(8,128)(2,1)} %bitcast.28), channel_id=1, source_target_pairs={{0,32},{32,64},{64,96},{96,0},{1,33},{33,65},{65,97},{97,1},{2,34}... | collective-permute-start | bytes 1966088 | tf_op jit(solution)/shard_map/ppermute | solution.py:104
  125.7 25.2 %collective-permute-start.12 = (bf16[256,1280]{1,0:T(8,128)(2,1)}, bf16[256,1280]{1,0:T(8,128)(2,1)}, u32[]{:S(2)}, u32[]{:S(2)}) collective-permute-start(bf16[256,1280]{1,0:T(8,128)(2,1)} %bitcast.28), channel_id=1, source_target_pairs={{0,96},{32,0},{64,32},{96,64},{1,97},{33,1},{65,33},{97,65},{2,98}... | collective-permute-start | bytes 1966088 | tf_op jit(solution)/shard_map/ppermute | solution.py:105
  144.6 52.9 %collective-permute-start.5 = (bf16[512,1280]{1,0:T(8,128)(2,1)}, bf16[512,1280]{1,0:T(8,128)(2,1)}, u32[]{:S(2)}, u32[]{:S(2)}) collective-permute-start(bf16[512,1280]{1,0:T(8,128)(2,1)} %bitcast.22), channel_id=1, source_target_pairs={{0,32},{32,64},{64,96},{96,0},{1,33},{33,65},{65,97},{97,1},{2,34}... | collective-permute-start | bytes 3932168 | tf_op jit(solution)/shard_map/ppermute | solution.py:104
  145.2 53.6 %collective-permute-start.4 = (bf16[512,1280]{1,0:T(8,128)(2,1)}, bf16[512,1280]{1,0:T(8,128)(2,1)}, u32[]{:S(2)}, u32[]{:S(2)}) collective-permute-start(bf16[512,1280]{1,0:T(8,128)(2,1)} %bitcast.22), channel_id=1, source_target_pairs={{0,96},{32,0},{64,32},{96,64},{1,97},{33,1},{65,33},{97,65},{2,98}... | collective-permute-start | bytes 3932168 | tf_op jit(solution)/shard_map/ppermute | solution.py:105
  148.3 34.9 %collective-permute-start.14 = (bf16[128,1280]{1,0:T(8,128)(2,1)S(1)}, bf16[128,1280]{1,0:T(8,128)(2,1)S(1)}, u32[]{:S(2)}, u32[]{:S(2)}) collective-permute-start(bf16[128,1280]{1,0:T(8,128)(2,1)S(1)} %slice.141), channel_id=1, source_target_pairs={{0,32},{32,64},{64,96},{96,0},{1,33},{33,65},{65,97},{97,1},{2,34}... | collective-permute-start | bytes 983048 | tf_op jit(solution)/shard_map/ppermute | solution.py:108
  151.9 32.1 %collective-permute-start.15 = (bf16[128,1280]{1,0:T(8,128)(2,1)S(1)}, bf16[128,1280]{1,0:T(8,128)(2,1)S(1)}, u32[]{:S(2)}, u32[]{:S(2)}) collective-permute-start(bf16[128,1280]{1,0:T(8,128)(2,1)S(1)} %slice.142), channel_id=1, source_target_pairs={{0,96},{32,0},{64,32},{96,64},{1,97},{33,1},{65,33},{97,65},{2,98}... | collective-permute-start | bytes 983048 | tf_op jit(solution)/shard_map/ppermute | solution.py:109
  198.7 16.5 %collective-permute-start.6 = (bf16[256,1280]{1,0:T(8,128)(2,1)S(1)}, bf16[256,1280]{1,0:T(8,128)(2,1)S(1)}, u32[]{:S(2)}, u32[]{:S(2)}) collective-permute-start(bf16[256,1280]{1,0:T(8,128)(2,1)S(1)} %slice.132), channel_id=1, source_target_pairs={{0,32},{32,64},{64,96},{96,0},{1,33},{33,65},{65,97},{97,1},{2,34}... | collective-permute-start | bytes 1966088 | tf_op jit(solution)/shard_map/ppermute | solution.py:108
  199.9 16.2 %collective-permute-start.7 = (bf16[256,1280]{1,0:T(8,128)(2,1)S(1)}, bf16[256,1280]{1,0:T(8,128)(2,1)S(1)}, u32[]{:S(2)}, u32[]{:S(2)}) collective-permute-start(bf16[256,1280]{1,0:T(8,128)(2,1)S(1)} %slice.133), channel_id=1, source_target_pairs={{0,96},{32,0},{64,32},{96,64},{1,97},{33,1},{65,33},{97,65},{2,98}... | collective-permute-start | bytes 1966088 | tf_op jit(solution)/shard_map/ppermute | solution.py:109
  205.0 37.9 %collective-permute-start.16 = (bf16[128,1280]{1,0:T(8,128)(2,1)}, bf16[128,1280]{1,0:T(8,128)(2,1)}, u32[]{:S(2)}, u32[]{:S(2)}) collective-permute-start(bf16[128,1280]{1,0:T(8,128)(2,1)} %get-tuple-element.17), channel_id=1, source_target_pairs={{0,32},{32,64},{64,96},{96,0},{1,33},{33,65},{65,97},{97,1},{2,34}... | collective-permute-start | bytes 983048 | tf_op jit(solution)/shard_map/ppermute | solution.py:118
  205.0 37.9 %collective-permute-start.18 = (bf16[128,1280]{1,0:T(8,128)(2,1)}, bf16[128,1280]{1,0:T(8,128)(2,1)}, u32[]{:S(2)}, u32[]{:S(2)}) collective-permute-start(bf16[128,1280]{1,0:T(8,128)(2,1)} %get-tuple-element.18), channel_id=1, source_target_pairs={{0,96},{32,0},{64,32},{96,64},{1,97},{33,1},{65,33},{97,65},{2,98}... | collective-permute-start | bytes 983048 | tf_op jit(solution)/shard_map/ppermute | solution.py:119
  238.0 4.9 %copy-start.5 = (bf16[1024,1280]{1,0:T(8,128)(2,1)S(1)}, bf16[1024,1280]{1,0:T(8,128)(2,1)}, u32[]{:S(2)}) copy-start(bf16[1024,1280]{1,0:T(8,128)(2,1)} %convolution_convert_fusion.1) | copy-start | bytes 7864324
  238.0 6.1 %copy-start.8 = (bf16[128,1280]{1,0:T(8,128)(2,1)S(1)}, bf16[128,1280]{1,0:T(8,128)(2,1)}, u32[]{:S(2)}) copy-start(bf16[128,1280]{1,0:T(8,128)(2,1)} %get-tuple-element.19) | copy-start | bytes 983044
  240.0 13.9 %collective-permute-start.8 = (bf16[256,1280]{1,0:T(8,128)(2,1)S(1)}, bf16[256,1280]{1,0:T(8,128)(2,1)S(1)}, u32[]{:S(2)}, u32[]{:S(2)}) collective-permute-start(bf16[256,1280]{1,0:T(8,128)(2,1)S(1)} %get-tuple-element.11), channel_id=1, source_target_pairs={{0,32},{32,64},{64,96},{96,0},{1,33},{33,65},{65,97},{97,1},{2,34}... | collective-permute-start | bytes 1966088 | tf_op jit(solution)/shard_map/ppermute | solution.py:118
  240.1 13.8 %collective-permute-start.10 = (bf16[256,1280]{1,0:T(8,128)(2,1)S(1)}, bf16[256,1280]{1,0:T(8,128)(2,1)S(1)}, u32[]{:S(2)}, u32[]{:S(2)}) collective-permute-start(bf16[256,1280]{1,0:T(8,128)(2,1)S(1)} %get-tuple-element.12), channel_id=1, source_target_pairs={{0,96},{32,0},{64,32},{96,64},{1,97},{33,1},{65,33},{97,65},{2,98}... | collective-permute-start | bytes 1966088 | tf_op jit(solution)/shard_map/ppermute | solution.py:119
  244.2 22.8 %collective-permute-start.19 = (bf16[256,1280]{1,0:T(8,128)(2,1)S(1)}, bf16[256,1280]{1,0:T(8,128)(2,1)S(1)}, u32[]{:S(2)}, u32[]{:S(2)}) collective-permute-start(bf16[256,1280]{1,0:T(8,128)(2,1)S(1)} %pad_maximum_fusion.5), channel_id=1, source_target_pairs={{0,96},{32,0},{64,32},{96,64},{1,97},{33,1},{65,33},{97,65},{2,98}... | collective-permute-start | bytes 1966088 | tf_op jit(solution)/shard_map/ppermute | solution.py:127
  255.5 4.8 %copy-start.7 = (bf16[128,1280]{1,0:T(8,128)(2,1)S(1)}, bf16[128,1280]{1,0:T(8,128)(2,1)}, u32[]{:S(2)}) copy-start(bf16[128,1280]{1,0:T(8,128)(2,1)} %get-tuple-element.20) | copy-start | bytes 983044
  256.7 56.2 %collective-permute-start.11 = (bf16[512,1280]{1,0:T(8,128)(2,1)}, bf16[512,1280]{1,0:T(8,128)(2,1)}, u32[]{:S(2)}, u32[]{:S(2)}) collective-permute-start(bf16[512,1280]{1,0:T(8,128)(2,1)} %pad_maximum_fusion.3), channel_id=1, source_target_pairs={{0,96},{32,0},{64,32},{96,64},{1,97},{33,1},{65,33},{97,65},{2,98}... | collective-permute-start | bytes 3932168 | tf_op jit(solution)/shard_map/ppermute | solution.py:127
  260.3 52.6 %collective-permute-start.9 = (bf16[512,1280]{1,0:T(8,128)(2,1)}, bf16[512,1280]{1,0:T(8,128)(2,1)S(1)}, u32[]{:S(2)}, u32[]{:S(2)}) collective-permute-start(bf16[512,1280]{1,0:T(8,128)(2,1)} %pad_maximum_fusion.2), channel_id=1, source_target_pairs={{0,32},{32,64},{64,96},{96,0},{1,33},{33,65},{65,97},{97,1},{2,34}... | collective-permute-start | bytes 3932168 | tf_op jit(solution)/shard_map/ppermute | solution.py:126
  260.4 36.1 %collective-permute-start.17 = (bf16[256,1280]{1,0:T(8,128)(2,1)S(1)}, bf16[256,1280]{1,0:T(8,128)(2,1)S(1)}, u32[]{:S(2)}, u32[]{:S(2)}) collective-permute-start(bf16[256,1280]{1,0:T(8,128)(2,1)S(1)} %pad_maximum_fusion.4), channel_id=1, source_target_pairs={{0,32},{32,64},{64,96},{96,0},{1,33},{33,65},{65,97},{97,1},{2,34}... | collective-permute-start | bytes 1966088 | tf_op jit(solution)/shard_map/ppermute | solution.py:126
  297.6 28.2 %all-to-all-start.4 = ((bf16[32,1,8,1280]{3,2,1,0:T(8,128)(2,1)}), bf16[32,1,8,1280]{3,2,1,0:T(8,128)(2,1)S(1)}, u32[]{:S(2)}, u32[]{:S(2)}) async-start(bf16[32,1,8,1280]{3,2,1,0:T(8,128)(2,1)} %fusion.62), calls=%async_computation.4 | async-start | bytes 1310720 | tf_op jit(solution)/shard_map/all_to_all | solution.py:132
  312.9 16.7 %copy-start.4 = (bf16[257,1280]{1,0:T(8,128)(2,1)S(1)}, bf16[257,1280]{1,0:T(8,128)(2,1)}, u32[]{:S(2)}) copy-start(bf16[257,1280]{1,0:T(8,128)(2,1)} %copy-done.3) | copy-start | bytes 1973764
  312.9 16.7 %copy-start.9 = (bf16[1280,32]{0,1:T(8,128)(2,1)S(1)}, bf16[1280,32]{0,1:T(8,128)(2,1)}, u32[]{:S(2)}) copy-start(bf16[1280,32]{0,1:T(8,128)(2,1)} %param.14) | copy-start | bytes 245764
  325.8 23.5 %all-to-all-start.2 = ((bf16[32,1,16,1280]{3,2,1,0:T(8,128)(2,1)}), bf16[32,1,16,1280]{3,2,1,0:T(8,128)(2,1)S(1)}, u32[]{:S(2)}, u32[]{:S(2)}) async-start(bf16[32,1,16,1280]{3,2,1,0:T(8,128)(2,1)} %bitcast.26), calls=%async_computation.2 | async-start | bytes 2621440 | tf_op jit(solution)/shard_map/all_to_all | solution.py:132
  (4 other events, 7.6 us)
